TPU v7x, 512 devices: a whole 4x4x16 slice. The times are simulated.
512 devices in a mesh: grp: 16 (over z), lat: 32 (over y, x, core).
Axes of the slice: x: 4, y: 4, z: 16, core: 2. Of those that a mesh axis runs over, the one named last changes fastest.
Arguments:
- stream: bfloat16 [256, 8192], P('lat'), may hold values from -26 to 26
- batch_index: int32 [256], replicated, may hold values from 0 to 255
- weight: bfloat16 [8192, 65536], P(None, ('grp', 'lat')), may hold values from -0.26516504 to 0.26516504
- enc_bias: float32 [65536], P(('grp', 'lat')), may hold values from -1.5 to 0.5
- dec_bias: float32 [8192], replicated, may hold values from -3 to 3
Outputs:
- weight_grad: bfloat16 [8192, 65536], P(None, ('grp', 'lat'))
- bias_grad: float32 [65536], P(('grp', 'lat'))
- recon_error: bfloat16 [256, 8192], P('lat')
All inputs are finite; a program needn't handle non-finite values.
Results may differ from a plain program's by a relative error of at most 0.025.
Values may be sent and summed in bfloat16 or wider, within the bound.
No kernel may reach another device: no remote copies, remote signals or barrier semaphores. Data moves between devices by JAX's collectives and lax.ppermute only.
A program may use at most 64 MiB of HBM per device.

v0:
```python
import jax
import jax.numpy as jnp
from jax import lax
from jax.sharding import PartitionSpec as P

sharpness = 8.0
penalty = 0.25
epsilon = 1e-06


def body(stream, batch_index, weight, enc_bias, dec_bias):
    own_rows = stream.shape[0]
    rank_lat = lax.axis_index("lat")
    gathered = lax.all_gather(stream, "lat", axis=0, tiled=True)
    batch = jnp.take(gathered, batch_index, axis=0)
    centered = (batch.astype(jnp.float32) - dec_bias).astype(jnp.bfloat16)
    preact = jnp.dot(centered, weight, preferred_element_type=jnp.float32) + enc_bias
    active = (jax.nn.softplus(sharpness * preact) / sharpness).astype(jnp.bfloat16)
    first_row = rank_lat * own_rows
    own_batch = lax.dynamic_slice_in_dim(batch, first_row, own_rows, 0)
    block_recon = lax.psum_scatter(
        lax.dot_general(
            active, weight, (((1,), (1,)), ((), ())), preferred_element_type=jnp.float32
        ).astype(jnp.bfloat16),
        "lat",
        scatter_dimension=0,
        tiled=True,
    )
    recon = lax.psum(block_recon, "grp").astype(jnp.float32)
    error_own = recon + dec_bias - own_batch.astype(jnp.float32)
    grad_own = (2.0 * error_own).astype(jnp.bfloat16)
    grad_rows = lax.all_gather(grad_own, "lat", axis=0, tiled=True)
    grad_active = jnp.dot(grad_rows, weight, preferred_element_type=jnp.float32)
    decoder_grad = lax.dot_general(
        grad_rows, active, (((0,), (0,)), ((), ())), preferred_element_type=jnp.float32
    )
    grad_pre = (grad_active + penalty) * jax.nn.sigmoid(sharpness * preact)
    encoder_grad = lax.dot_general(
        centered,
        grad_pre.astype(jnp.bfloat16),
        (((0,), (0,)), ((), ())),
        preferred_element_type=jnp.float32,
    )
    grad_raw = encoder_grad + decoder_grad
    bias_raw = jnp.sum(grad_pre, axis=0)
    local_squares = jnp.sum(grad_raw * grad_raw) + jnp.sum(bias_raw * bias_raw)
    total_squares = lax.psum(local_squares, ("grp", "lat"))
    entries = (weight.shape[0] + 1) * weight.shape[1] * lax.axis_size("lat") * lax.axis_size("grp")
    factor = jnp.minimum(1.0, 1.0 / jnp.sqrt(total_squares / entries + epsilon))
    return (
        (grad_raw * factor).astype(jnp.bfloat16),
        bias_raw * factor,
        error_own.astype(jnp.bfloat16),
    )


def solution(mesh):
    return jax.shard_map(
        body,
        mesh=mesh,
        in_specs=(P("lat", None), P(), P(None, ("grp", "lat")), P(("grp", "lat")), P()),
        out_specs=(P(None, ("grp", "lat")), P(("grp", "lat")), P("lat", None)),
        check_vma=False,
    )
```

profile of v0, /device:TPU:1, one launch (start us, length us, event | category | flops | bytes accessed | tf_op | source)
XLA Modules:
  0.0 528.7 jit_solution(4097323418237096294)
XLA Ops:
  7.2 0.7 all-gather.3.cloned.1.call-update
  7.9 0.0 reduce-scatter.2.cloned.1.call-start
  8.0 0.7 compare_select_fusion.1
  8.7 0.7 compare_and_fusion
  9.3 68.9 %all-gather.3.cloned.1.call-done = bf16[256,8192]{1,0:T(8,128)(2,1)} async-done(((bf16[8,8192]{1,0:T(8,128)(2,1)}), bf16[256,8192]{1,0:T(8,128)(2,1)}) %all-gather.3.cloned.1.call-update) | async-done | bytes 4194320 | tf_op jit(solution)/shard_map/all_gather | solution.py:14
  78.3 11.7 %gather_fusion = bf16[256,8192]{1,0:T(8,128)(2,1)} fusion(bf16[256,8192]{1,0:T(8,128)(2,1)} %all-gather.3.cloned.1.call-done, s32[1024]{0:T(1024)S(1)} %pad_clamp_fusion), kind=kCustom, calls=%fused_computation | custom fusion | bytes 8389632 | tf_op jit(solution)/shard_map/jit(_take)/gather | solution.py:15
  90.0 2.7 broadcast_select_fusion
  92.7 1.9 copy-done.1
  94.6 1.3 fusion.4
  95.9 3.2 convolution_convert_fusion
  99.2 0.0 all-reduce.2.cloned.1.call-start
  99.2 102.6 %reduce-scatter.2.cloned.1.call-done = bf16[8,8192]{1,0:T(8,128)(2,1)} async-done(((bf16[256,8192]{1,0:T(8,128)(2,1)}), bf16[8,8192]{1,0:T(8,128)(2,1)}) %reduce-scatter.2.cloned.1.call-update) | async-done | bytes 131088 | tf_op jit(solution)/shard_map/reduce_scatter | solution.py:21
  201.8 0.2 all-gather.5.cloned.1.call-start
  202.0 128.7 %all-reduce.2.cloned.1.call-done = bf16[8,8192]{1,0:T(8,128)(2,1)} async-done(((bf16[8,8192]{1,0:T(8,128)(2,1)}), bf16[8,8192]{1,0:T(8,128)(2,1)}) %all-reduce.2.cloned.1.call-update) | async-done | bytes 131088 | tf_op jit(solution)/shard_map/psum | solution.py:29
  330.7 1.7 fusion.5
  332.5 69.7 %all-gather.5.cloned.1.call-done = bf16[256,8192]{1,0:T(8,128)(2,1)} async-done(((bf16[8,8192]{1,0:T(8,128)(2,1)}), bf16[256,8192]{1,0:T(8,128)(2,1)}) %all-gather.5.cloned.1.call-update) | async-done | bytes 4194320 | tf_op jit(solution)/shard_map/all_gather | solution.py:32
  402.2 3.6 fusion.11
  405.8 1.5 fusion
  407.3 0.6 multiply_reduce_fusion.1
  407.9 0.1 copy-done.3
  408.0 4.4 multiply_reduce_fusion
  413.6 103.6 %psum.15 = f32[]{:T(128)} all-reduce(f32[]{:T(128)S(6)} %add.67), channel_id=1, replica_groups=mesh['grp'=16,'lat'=32] {'grp','lat'}, use_global_device_ids=true, to_apply=%region_5.6 | all-reduce | flops 1 | bytes 8 | tf_op jit(solution)/shard_map/psum | solution.py:47
  518.0 0.5 broadcast_multiply_fusion
  518.5 3.7 multiply_convert_fusion
  (15 shorter events, 0.1 us)
Async XLA Ops:
  7.2 87.4 %copy-start = (bf16[8192,128]{1,0:T(8,128)(2,1)S(1)}, bf16[8192,128]{1,0:T(8,128)(2,1)}, u32[]{:S(2)}) copy-start(bf16[8192,128]{1,0:T(8,128)(2,1)} %param.7) | copy-start | bytes 6291460
  7.2 71.1 %all-gather.3.cloned.1.call-start = ((), (), s32[]{:S(2)}) async-start(), calls=%async_computation.1 | async-start | bytes 4325376 | tf_op jit(solution)/shard_map/all_gather | solution.py:14
  7.9 193.9 %reduce-scatter.2.cloned.1.call-start = ((), (), s32[]{:S(2)}) async-start(), calls=%async_computation.2 | async-start | bytes 4325376 | tf_op jit(solution)/shard_map/reduce_scatter | solution.py:21
  90.0 4.6 copy-start.4
  90.0 4.6 copy-start.5
  92.6 1.9 copy-start.1
  99.2 231.6 %all-reduce.2.cloned.1.call-start = ((), (), s32[]{:S(2)}) async-start(), calls=%async_computation.3 | async-start | bytes 262144 | tf_op jit(solution)/shard_map/psum | solution.py:29
  201.8 200.4 %all-gather.5.cloned.1.call-start = ((), (), s32[]{:S(2)}) async-start(), calls=%async_computation.4 | async-start | bytes 4325376 | tf_op jit(solution)/shard_map/all_gather | solution.py:32
  402.2 3.6 copy-start.2
  405.8 2.2 copy-start.3
Sparse Core Ops, SparseCore 0:
  11.1 67.0 all-gather.2
  99.3 102.4 reduce-scatter.1
  204.2 126.4 all-reduce.1
  334.3 67.8 all-gather.4
where the time goes:
time: 529 us
  waiting for transfers between devices  371 us (70%)
  blocking collectives  104 us (20%)
  between operations  15.8 us (3%)
  matrix products  14 us (3%)
  local copies, waits for them, and re-layouts  13.7 us (3%)
  other arithmetic  10.6 us (2%)
    psum x1, waiting for transfers between devices, body(): recon = lax.psum(block_recon, 'grp').astype(jnp.float32)  129 us
    psum x1, blocking collectives, body(): total_squares = lax.psum(local_squares, ('grp', 'lat'))  104 us
    reduce_scatter x1, waiting for transfers between devices, body(): lax.psum_scatter(lax.dot_general(active, weight, (((1,), (1,)), ((), ()))...  103 us
    all_gather x1, waiting for transfers between devices, body(): grad_rows = lax.all_gather(grad_own, 'lat', axis=0, tiled=True)  69.7 us
    all_gather x1, waiting for transfers between devices, body(): gathered = lax.all_gather(stream, 'lat', axis=0, tiled=True)  68.9 us
    gather x1, local copies, waits for them, and re-layouts, body(): batch = jnp.take(gathered, batch_index, axis=0)  11.7 us
  transfers between devices with their start and end apart: 4, of which 4 were waited for; matrix products, arithmetic and copies ran while one was open for 0% of the time, Pallas kernels for 0%

commit v1 on v0

--- a/solution.py
+++ b/solution.py
@@ -26,7 +26,10 @@
         scatter_dimension=0,
         tiled=True,
     )
-    recon = lax.psum(block_recon, "grp").astype(jnp.float32)
+    read_the_desk = lambda state, which_axis: lax.all_gather(state, axis_name=which_axis).sum(
+        axis=0
+    )
+    recon = read_the_desk(block_recon, "grp").astype(jnp.float32)
     error_own = recon + dec_bias - own_batch.astype(jnp.float32)
     grad_own = (2.0 * error_own).astype(jnp.bfloat16)
     grad_rows = lax.all_gather(grad_own, "lat", axis=0, tiled=True)

time: 529 us -> 468 us (0.88)
  waiting for transfers between devices: 371 us -> 308 us
    psum x1 -> x0, waiting for transfers between devices: 129 us -> none  [body(): recon = lax.psum(block_recon, 'grp').astype(jnp.float32)]
    all_gather x0 -> x1, waiting for transfers between devices: none -> 67.2 us  [body(): lax.all_gather(state, axis_name=which_axis).sum(axis=0)]
where the time goes in v1:
time: 468 us
  waiting for transfers between devices  308 us (66%)
  blocking collectives  104 us (22%)
  between operations  15.8 us (3%)
  matrix products  14 us (3%)
  local copies, waits for them, and re-layouts  13.7 us (3%)
  other arithmetic  12.4 us (3%)
    psum x1, blocking collectives, body(): total_squares = lax.psum(local_squares, ('grp', 'lat'))  104 us
    reduce_scatter x1, waiting for transfers between devices, body(): lax.psum_scatter(lax.dot_general(active, weight, (((1,), (1,)), ((), ()))...  103 us
    all_gather x1, waiting for transfers between devices, body(): gathered = lax.all_gather(stream, 'lat', axis=0, tiled=True)  68.9 us
    all_gather x1, waiting for transfers between devices, body(): grad_rows = lax.all_gather(grad_own, 'lat', axis=0, tiled=True)  68.3 us
    all_gather x1, waiting for transfers between devices, body(): lax.all_gather(state, axis_name=which_axis).sum(axis=0)  67.2 us
    gather x1, local copies, waits for them, and re-layouts, body(): batch = jnp.take(gathered, batch_index, axis=0)  11.7 us
  transfers between devices with their start and end apart: 4, of which 4 were waited for; matrix products, arithmetic and copies ran while one was open for 0% of the time, Pallas kernels for 0%

profile of v1, /device:TPU:1, one launch (start us, length us, event | category | flops | bytes accessed | tf_op | source)
XLA Modules:
  0.0 467.7 jit_solution(14080454699518466450)
XLA Ops:
  7.2 0.7 all-gather.5.cloned.1.call-update
  8.0 0.7 compare_select_fusion.1
  8.7 0.7 compare_and_fusion
  9.3 68.9 %all-gather.5.cloned.1.call-done = bf16[256,8192]{1,0:T(8,128)(2,1)} async-done(((bf16[8,8192]{1,0:T(8,128)(2,1)}), bf16[256,8192]{1,0:T(8,128)(2,1)}) %all-gather.5.cloned.1.call-update) | async-done | bytes 4194320 | tf_op jit(solution)/shard_map/all_gather | solution.py:14
  78.3 11.7 %gather_fusion = bf16[256,8192]{1,0:T(8,128)(2,1)} fusion(bf16[256,8192]{1,0:T(8,128)(2,1)} %all-gather.5.cloned.1.call-done, s32[1024]{0:T(1024)S(1)} %pad_clamp_fusion), kind=kCustom, calls=%fused_computation | custom fusion | bytes 8389632 | tf_op jit(solution)/shard_map/jit(_take)/gather | solution.py:15
  90.0 2.7 broadcast_select_fusion
  92.7 1.9 copy-done.1
  94.6 1.3 fusion.4
  95.9 3.2 convolution_convert_fusion
  99.2 0.0 all-gather.9.cloned.1.call-start
  99.2 102.6 %reduce-scatter.2.cloned.1.call-done = bf16[8,8192]{1,0:T(8,128)(2,1)} async-done(((bf16[256,8192]{1,0:T(8,128)(2,1)}), bf16[8,8192]{1,0:T(8,128)(2,1)}) %reduce-scatter.2.cloned.1.call-update) | async-done | bytes 131088 | tf_op jit(solution)/shard_map/reduce_scatter | solution.py:21
  201.8 0.2 all-gather.7.cloned.1.call-start
  202.0 67.2 %all-gather.9.cloned.1.call-done = bf16[128,8192]{1,0:T(8,128)(2,1)} async-done(((bf16[8,8192]{1,0:T(8,128)(2,1)}), bf16[128,8192]{1,0:T(8,128)(2,1)}) %all-gather.9.cloned.1.call-update) | async-done | bytes 2097168 | tf_op jit(solution)/shard_map/all_gather | solution.py:29
  269.3 1.9 bitcast_reduce_fusion
  271.1 1.7 fusion.5
  272.8 68.3 %all-gather.7.cloned.1.call-done = bf16[256,8192]{1,0:T(8,128)(2,1)} async-done(((bf16[8,8192]{1,0:T(8,128)(2,1)}), bf16[256,8192]{1,0:T(8,128)(2,1)}) %all-gather.7.cloned.1.call-update) | async-done | bytes 4194320 | tf_op jit(solution)/shard_map/all_gather | solution.py:35
  341.2 3.6 fusion.11
  344.8 1.5 fusion
  346.3 0.6 multiply_reduce_fusion.1
  346.9 0.1 copy-done.3
  347.0 4.4 multiply_reduce_fusion
  352.6 103.6 %psum.7 = f32[]{:T(128)} all-reduce(f32[]{:T(128)S(6)} %add.65), channel_id=1, replica_groups=mesh['grp'=16,'lat'=32] {'grp','lat'}, use_global_device_ids=true, to_apply=%region_5.6 | all-reduce | flops 1 | bytes 8 | tf_op jit(solution)/shard_map/psum | solution.py:50
  456.9 0.5 broadcast_multiply_fusion
  457.5 3.7 multiply_convert_fusion
  (16 shorter events, 0.2 us)
Async XLA Ops:
  7.2 87.4 %copy-start = (bf16[8192,128]{1,0:T(8,128)(2,1)S(1)}, bf16[8192,128]{1,0:T(8,128)(2,1)}, u32[]{:S(2)}) copy-start(bf16[8192,128]{1,0:T(8,128)(2,1)} %param.7) | copy-start | bytes 6291460
  7.2 71.1 %all-gather.5.cloned.1.call-start = ((), (), s32[]{:S(2)}) async-start(), calls=%async_computation.1 | async-start | bytes 4325376 | tf_op jit(solution)/shard_map/all_gather | solution.py:14
  7.9 193.9 %reduce-scatter.2.cloned.1.call-start = ((), (), s32[]{:S(2)}) async-start(), calls=%async_computation.2 | async-start | bytes 4325376 | tf_op jit(solution)/shard_map/reduce_scatter | solution.py:21
  90.0 4.6 copy-start.4
  90.0 4.6 copy-start.5
  92.6 1.9 copy-start.1
  99.2 170.1 %all-gather.9.cloned.1.call-start = ((), (), s32[]{:S(2)}) async-start(), calls=%async_computation.4 | async-start | bytes 2228224 | tf_op jit(solution)/shard_map/all_gather | solution.py:29
  201.8 139.4 %all-gather.7.cloned.1.call-start = ((), (), s32[]{:S(2)}) async-start(), calls=%async_computation.3 | async-start | bytes 4325376 | tf_op jit(solution)/shard_map/all_gather | solution.py:35
  341.2 3.6 copy-start.2
  344.8 2.2 copy-start.3
Sparse Core Ops, SparseCore 0:
  11.1 67.0 all-gather.4
  99.3 102.4 reduce-scatter.1
  204.1 65.1 all-gather.8
  273.3 67.8 all-gather.6
